TPU v7x, 256 devices: a whole 4x4x8 slice. The times are simulated.
256 devices in a mesh: fsdp: 8 (over z_lo, core), seq: 32 (over x, z_hi, y).
Axes of the slice: x: 4, y: 4, z: 8 (z_hi: 2, z_lo: 4; z = z_hi * 4 + z_lo), core: 2. Of those that a mesh axis runs over, the one named last changes fastest.
Arguments:
- tokens: bfloat16 [2, 4096, 4096], P(None, 'seq'), may hold values from -6 to 6
- positions: int32 [2, 4096], replicated, may hold values from 0 to 4095, as said below
- cached_len: int32 [2], replicated, may hold values from 16 to 4096, as said below
- cache_keys: bfloat16 [2, 4096, 8, 128], P(None, 'seq', 'fsdp'), may hold values from -6 to 6
- cache_values: bfloat16 [2, 4096, 8, 128], P(None, 'seq', 'fsdp'), may hold values from -6 to 6
- w_query: bfloat16 [4096, 4096], P('seq', 'fsdp')
- w_key: bfloat16 [4096, 1024], P('seq', 'fsdp')
- w_value: bfloat16 [4096, 1024], P('seq', 'fsdp'), may hold values from -0.09375 to 0.09375
- w_out_t: bfloat16 [4096, 4096], P('seq', 'fsdp'), may hold values from -1.5 to 1.5
Outputs:
- mixed: bfloat16 [2, 4096, 4096], P(None, 'seq', 'fsdp')
- new_keys: bfloat16 [2, 4096, 8, 128], P(None, 'seq', 'fsdp')
- new_values: bfloat16 [2, 4096, 8, 128], P(None, 'seq', 'fsdp')
Inputs may be any that keep to these rules, and one draw needn't show every extreme that they name: For each request the stored order is a permutation of 0 to 4095: the span is cut into 64 blocks of 64 positions, and the 128 stored rows of each index of seq are one block b followed by the block 63 - b, each in rising order; b is drawn per request and index. `cached_len`: some request has exactly 4096 cached positions.
All inputs are finite; a program needn't handle non-finite values.
Results may differ from a plain program's by a relative error of at most 0.015.
The roundings to bfloat16 on the way count: a program that leaves them out, or rounds other values in their place, can miss the bound.
Values may be sent and summed in bfloat16 or wider, within the bound.
No kernel may reach another device: no remote copies, remote signals or barrier semaphores. Data moves between devices by JAX's collectives and lax.ppermute only.
A program may use at most 128 MiB of HBM per device.

v0:
```python
import math
import jax
import jax.numpy as jnp
from jax import lax
from jax.sharding import PartitionSpec as P

SINKS = 4
NEGATIVE = -1e30


def attend_block(running_state, queries, key_block, value_block, allowed):
    top_old, denom_old, numer_old = running_state
    scores = jnp.einsum("rqkgd,rpkd->rkgqp", queries, key_block, preferred_element_type=jnp.float32)
    scores = scores * (1.0 / math.sqrt(queries.shape[-1]))
    visible = allowed[:, None, None, :, :]
    scores = jnp.where(visible, scores, NEGATIVE)
    top_new = jnp.maximum(top_old, jnp.max(scores, axis=-1))
    rescale = jnp.exp(top_old - top_new)
    weights = jnp.where(visible, jnp.exp(scores - top_new[..., None]), 0.0)
    denom_new = denom_old * rescale + jnp.sum(weights, axis=-1)
    numer_new = numer_old * rescale[..., None] + jnp.einsum(
        "rkgqp,rpkd->rkgqd",
        weights.astype(jnp.bfloat16),
        value_block,
        preferred_element_type=jnp.float32,
    )
    return (top_new, denom_new, numer_new)


def shards(
    tokens, positions, cached_len, cache_keys, cache_values, w_query, w_key, w_value, w_out_t
):
    requests, rows, width = tokens.shape
    head_size = cache_keys.shape[3]
    kv_local = cache_keys.shape[2]
    group_size = w_query.shape[1] // (kv_local * head_size)
    seq_index = lax.axis_index("seq")
    seq_count = lax.axis_size("seq")
    window_len = rows * seq_count // 2
    my_positions = lax.dynamic_slice_in_dim(positions, seq_index * rows, rows, 1)
    flat_tokens = tokens.reshape(requests * rows, width)
    weight_pieces = (
        lax.all_gather(w_query, "seq", axis=0, tiled=True),
        lax.all_gather(w_key, "seq", axis=0, tiled=True),
        lax.all_gather(w_value, "seq", axis=0, tiled=True),
    )
    query_sum, key_sum, value_sum = tuple(
        (
            jnp.dot(flat_tokens, weight_piece, preferred_element_type=jnp.float32)
            for weight_piece in weight_pieces
        )
    )
    queries = query_sum.astype(jnp.bfloat16).reshape(
        requests, rows, kv_local, group_size, head_size
    )
    new_keys = key_sum.astype(jnp.bfloat16).reshape(requests, rows, kv_local, head_size)
    new_values = value_sum.astype(jnp.bfloat16).reshape(requests, rows, kv_local, head_size)
    lengths = cached_len[:, None]
    window_floor = lengths + my_positions - window_len
    running_state = (
        jnp.full((requests, kv_local, group_size, rows), NEGATIVE, jnp.float32),
        jnp.zeros((requests, kv_local, group_size, rows), jnp.float32),
        jnp.zeros((requests, kv_local, group_size, rows, head_size), jnp.float32),
    )
    block_pieces = (
        lax.all_gather(cache_keys, "seq", axis=1, tiled=True),
        lax.all_gather(cache_values, "seq", axis=1, tiled=True),
    )
    key_pos = jnp.arange(block_pieces[0].shape[1], dtype=jnp.int32)
    key_pos = key_pos[None, None, :]
    allowed = (key_pos < lengths[:, :, None]) & (
        (key_pos < SINKS) | (key_pos > window_floor[:, :, None])
    )
    running_state = attend_block(running_state, queries, block_pieces[0], block_pieces[1], allowed)
    block_pieces = (
        lax.all_gather(new_keys, "seq", axis=1, tiled=True),
        lax.all_gather(new_values, "seq", axis=1, tiled=True),
    )
    before = my_positions[:, :, None] - positions[:, None, :]
    allowed = (before >= 0) & (before < window_len)
    running_state = attend_block(running_state, queries, block_pieces[0], block_pieces[1], allowed)
    top_final, denom_final, numer_final = running_state
    attended = (numer_final / denom_final[..., None]).astype(jnp.bfloat16)
    attended = jnp.transpose(attended, (0, 3, 1, 2, 4)).reshape(
        requests * rows, kv_local * group_size * head_size
    )
    partial_out = lax.dot_general(
        attended,
        lax.all_gather(w_out_t, "seq", axis=0, tiled=True),
        (((1,), (1,)), ((), ())),
        preferred_element_type=jnp.float32,
    )
    mixed = lax.psum_scatter(
        partial_out.reshape(requests, rows, width).astype(jnp.bfloat16),
        "fsdp",
        scatter_dimension=2,
        tiled=True,
    )
    return (mixed, new_keys, new_values)


def solution(mesh):
    placed = (
        P(None, "seq", None),
        P(),
        P(),
        P(None, "seq", "fsdp", None),
        P(None, "seq", "fsdp", None),
        P("seq", "fsdp"),
        P("seq", "fsdp"),
        P("seq", "fsdp"),
        P("seq", "fsdp"),
    )
    return jax.shard_map(
        shards,
        mesh=mesh,
        in_specs=placed,
        out_specs=(
            P(None, "seq", "fsdp"),
            P(None, "seq", "fsdp", None),
            P(None, "seq", "fsdp", None),
        ),
        check_vma=False,
    )
```

profile of v0, /device:TPU:6, one launch (start us, length us, event | category | flops | bytes accessed | tf_op | source)
XLA Modules:
  0.0 814.5 jit_solution(16966259465033407726)
XLA Ops:
  7.2 0.7 all-gather.15.cloned.1.call-update
  8.0 0.7 all-gather.19.cloned.1.call-update
  8.7 0.7 all-gather.9.cloned.1.call-update
  9.4 84.8 %all-gather.15.cloned.1.call-done = bf16[4096,128]{1,0:T(8,128)(2,1)} async-done(((bf16[128,128]{1,0:T(8,128)(2,1)}), bf16[4096,128]{1,0:T(8,128)(2,1)}) %all-gather.15.cloned.1.call-update) | async-done | bytes 1048592 | tf_op jit(solution)/shard_map/all_gather | solution.py:44
  94.2 2.6 convolution_convert_fusion.3
  96.8 0.0 all-gather.11.cloned.1.call-start
  96.8 0.5 all-gather.11.cloned.1.call-update
  97.4 1.6 copy.14
  99.0 0.0 all-gather.21.cloned.1.call-start
  99.1 74.3 %all-gather.19.cloned.1.call-done = bf16[4096,128]{1,0:T(8,128)(2,1)} async-done(((bf16[128,128]{1,0:T(8,128)(2,1)}), bf16[4096,128]{1,0:T(8,128)(2,1)}) %all-gather.19.cloned.1.call-update) | async-done | bytes 1048592 | tf_op jit(solution)/shard_map/all_gather | solution.py:45
  173.3 1.9 convolution_convert_fusion.2
  175.3 0.7 copy.17
  176.1 0.7 all-gather.23.cloned.1.call-update
  176.9 0.7 iota_compare_fusion.1
  177.6 0.8 add_add_fusion
  178.4 3.5 fusion.16
  181.9 100.4 %all-gather.9.cloned.1.call-done = bf16[4096,512]{1,0:T(8,128)(2,1)} async-done(((bf16[128,512]{1,0:T(8,128)(2,1)}), bf16[4096,512]{1,0:T(8,128)(2,1)}) %all-gather.9.cloned.1.call-update) | async-done | bytes 4194320 | tf_op jit(solution)/shard_map/all_gather | solution.py:43
  282.3 4.1 convolution_convert_fusion.1
  286.4 1.0 reshape.173
  287.4 84.5 %all-gather.17.cloned.1.call-done = bf16[2,4096,1,128]{3,1,0,2:T(8,128)(2,1)} async-done(((bf16[2,128,1,128]{3,1,0,2:T(8,128)(2,1)}), bf16[2,4096,1,128]{3,1,0,2:T(8,128)(2,1)}) %all-gather.17.cloned.1.call-update) | async-done | bytes 2097168 | tf_op jit(solution)/shard_map/all_gather | solution.py:76
  371.9 9.3 %fusion.1 = (f32[2,4,128]{2,1,0:T(4,128)S(1)}, f32[2,4096,128,4]{1,2,3,0:T(8,128)}) fusion(pred[2,128,4096]{2,1,0:T(8,128)(4,1)S(1)} %get-tuple-element.18, bf16[2,128,4,128]{3,2,1,0:T(4,128)(2,1)S(1)} %reshape.173, bf16[2,4096,1,128]{3,1,0,2:T(8,128)(2,1)} %all-gather.17.cloned.1.call-done), kind=kOutput, calls=%fused_computation.5 | convolution fusion | flops 1086323712 | bytes 20189184 | tf_op jit(solution)/shard_map/rqkgd,rpkd->rkgqp/dot_general | solution.py:13
  381.2 79.6 %all-gather.11.cloned.1.call-done = bf16[2,4096,1,128]{3,1,0,2:T(8,128)(2,1)} async-done(((bf16[2,128,1,128]{3,1,0,2:T(8,128)(2,1)}), bf16[2,4096,1,128]{3,1,0,2:T(8,128)(2,1)}) %all-gather.11.cloned.1.call-update) | async-done | bytes 2097168 | tf_op jit(solution)/shard_map/all_gather | solution.py:66
  460.8 10.4 %fusion = (f32[2,4,128]{2,1,0:T(4,128)S(1)}, f32[2,128,4,4096]{3,1,2,0:T(8,128)}) fusion(pred[2,128,4096]{2,1,0:T(8,128)(4,1)} %get-tuple-element.17, bf16[2,4096,1,128]{3,1,0,2:T(8,128)(2,1)} %all-gather.11.cloned.1.call-done, bf16[2,128,4,128]{3,2,1,0:T(4,128)(2,1)S(1)} %reshape.173), kind=kOutput, calls=%fused_computation.4 | convolution fusion | flops 1086323712 | bytes 20189184 | tf_op jit(solution)/shard_map/rqkgd,rpkd->rkgqp/dot_general | solution.py:13
  471.2 8.7 %fusion.2 = f32[2,4,128]{2,1,0:T(4,128)S(1)} fusion(f32[2,128,4,4096]{3,1,2,0:T(8,128)} %get-tuple-element.14, f32[2,4,128]{2,1,0:T(4,128)S(1)} %get-tuple-element.12, pred[2,128,4096]{2,1,0:T(8,128)(4,1)S(1)} %copy-done.1), kind=kLoop, calls=%fused_computation.6 | loop fusion | flops 20970496 | bytes 17833984 | tf_op jit(solution)/shard_map/reduce_sum | solution.py:20
  479.9 5.0 fusion.4
  484.9 72.1 %all-gather.13.cloned.1.call-done = bf16[2,4096,1,128]{1,3,0,2:T(8,128)(2,1)} async-done(((bf16[2,128,1,128]{1,3,0,2:T(8,128)(2,1)}), bf16[2,4096,1,128]{1,3,0,2:T(8,128)(2,1)}) %all-gather.13.cloned.1.call-update) | async-done | bytes 2097168 | tf_op jit(solution)/shard_map/all_gather | solution.py:67
  557.0 10.6 %fusion.34 = f32[2,4,128,128]{2,3,1,0:T(8,128)} fusion(bf16[2,4096,1,128]{1,3,0,2:T(8,128)(2,1)} %all-gather.13.cloned.1.call-done, f32[2,128,4,4096]{3,1,2,0:T(8,128)} %get-tuple-element.14, f32[2,4,128]{2,1,0:T(4,128)S(1)} %get-tuple-element.12, pred[2,128,4096]{2,1,0:T(8,128)(4,1)} %get-tuple-element.17, f32[2,4,128]{2,1,0:T(4,128)S(1)} %get-tuple-element.7, ...), kind=kOutput, calls=%fused_computation.32 | convolution fusion | flops 1094975488 | bytes 20459520 | tf_op jit(solution)/shard_map/rkgqp,rpkd->rkgqd/dot_general | solution.py:21
  567.7 87.5 %all-gather.21.cloned.1.call-done = bf16[2,4096,1,128]{1,3,0,2:T(8,128)(2,1)} async-done(((bf16[2,128,1,128]{1,3,0,2:T(8,128)(2,1)}), bf16[2,4096,1,128]{1,3,0,2:T(8,128)(2,1)}) %all-gather.21.cloned.1.call-update) | async-done | bytes 2097168 | tf_op jit(solution)/shard_map/all_gather | solution.py:77
  655.1 9.7 %fusion.44 = bf16[2,4,128,128]{2,3,1,0:T(8,128)(2,1)S(1)} fusion(f32[2,4,128,128]{2,3,1,0:T(8,128)} %fusion.34, bf16[2,4096,1,128]{1,3,0,2:T(8,128)(2,1)} %all-gather.21.cloned.1.call-done, f32[2,4096,128,4]{1,2,3,0:T(8,128)} %get-tuple-element.16, f32[2,4,128]{2,1,0:T(4,128)S(1)} %get-tuple-element.11, pred[2,128,4096]{2,1,0:T(8,128)(4,1)S(1)} %get-tuple-element.18, ...), kind=kOutput, calls=%fused_computation.37 | convolution fusion | flops 1095106560 | bytes 20717568 | tf_op jit(solution)/shard_map/rkgqp,rpkd->rkgqd/dot_general | solution.py:21
  664.9 100.7 %all-gather.23.cloned.1.call-done = bf16[4096,512]{1,0:T(8,128)(2,1)} async-done(((bf16[128,512]{1,0:T(8,128)(2,1)}), bf16[4096,512]{1,0:T(8,128)(2,1)}) %all-gather.23.cloned.1.call-update) | async-done | bytes 4194320 | tf_op jit(solution)/shard_map/all_gather | solution.py:89
  765.6 4.8 convolution_convert_fusion
  770.5 37.5 %reduce-scatter.2.cloned.1.call-done = bf16[2,128,512]{2,1,0:T(8,128)(2,1)} async-done(((bf16[2,128,4096]{2,1,0:T(8,128)(2,1)}), bf16[2,128,512]{2,1,0:T(8,128)(2,1)}) %reduce-scatter.2.cloned.1.call-update) | async-done | bytes 262160 | tf_op jit(solution)/shard_map/reduce_scatter | solution.py:93
  (29 shorter events, 0.4 us)
Async XLA Ops:
  7.2 87.0 %copy-start = (bf16[2,128,4096]{2,1,0:T(8,128)(2,1)S(1)}, bf16[2,128,4096]{2,1,0:T(8,128)(2,1)}, u32[]{:S(2)}) copy-start(bf16[2,128,4096]{2,1,0:T(8,128)(2,1)} %param.9) | copy-start | bytes 6291460
  7.2 87.0 %all-gather.15.cloned.1.call-start = ((), (), s32[]{:S(2)}) async-start(), calls=%async_computation.4 | async-start | bytes 1081344 | tf_op jit(solution)/shard_map/all_gather | solution.py:44
  7.9 165.4 %all-gather.19.cloned.1.call-start = ((), (), s32[]{:S(2)}) async-start(), calls=%async_computation.6 | async-start | bytes 1081344 | tf_op jit(solution)/shard_map/all_gather | solution.py:45
  8.7 273.6 %all-gather.9.cloned.1.call-start = ((), (), s32[]{:S(2)}) async-start(), calls=%async_computation.1 | async-start | bytes 4325376 | tf_op jit(solution)/shard_map/all_gather | solution.py:43
  9.4 362.5 %all-gather.17.cloned.1.call-start = ((), (), s32[]{:S(2)}) async-start(), calls=%async_computation.5 | async-start | bytes 2162688 | tf_op jit(solution)/shard_map/all_gather | solution.py:76
  96.8 364.0 %all-gather.11.cloned.1.call-start = ((), (), s32[]{:S(2)}) async-start(), calls=%async_computation.2 | async-start | bytes 2162688 | tf_op jit(solution)/shard_map/all_gather | solution.py:66
  97.4 459.7 %all-gather.13.cloned.1.call-start = ((), (), s32[]{:S(2)}) async-start(), calls=%async_computation.3 | async-start | bytes 2162688 | tf_op jit(solution)/shard_map/all_gather | solution.py:67
  99.0 556.1 %all-gather.21.cloned.1.call-start = ((), (), s32[]{:S(2)}) async-start(), calls=%async_computation.7 | async-start | bytes 2162688 | tf_op jit(solution)/shard_map/all_gather | solution.py:77
  175.3 205.9 %copy-start.2 = (bf16[256,128]{1,0:T(8,128)(2,1)}, bf16[256,128]{1,0:T(8,128)(2,1)S(1)}, u32[]{:S(2)}) copy-start(bf16[256,128]{1,0:T(8,128)(2,1)S(1)} %convolution_convert_fusion.2) | copy-start | bytes 196612
  176.0 589.6 %all-gather.23.cloned.1.call-start = ((), (), s32[]{:S(2)}) async-start(), calls=%async_computation.8 | async-start | bytes 4325376 | tf_op jit(solution)/shard_map/all_gather | solution.py:89
  176.8 631.2 %reduce-scatter.2.cloned.1.call-start = ((), (), s32[]{:S(2)}) async-start(), calls=%async_computation.9 | async-start | bytes 2359296 | tf_op jit(solution)/shard_map/reduce_scatter | solution.py:93
  460.8 10.4 %copy-start.1 = (pred[2,128,4096]{2,1,0:T(8,128)(4,1)S(1)}, pred[2,128,4096]{2,1,0:T(8,128)(4,1)}, u32[]{:S(2)}) copy-start(pred[2,128,4096]{2,1,0:T(8,128)(4,1)} %get-tuple-element.17) | copy-start | bytes 3145732
  460.8 19.1 %slice-start = ((s8[16777216]{0:T(1024)(128)(4,1)}), s8[4194304]{0:T(1024)(128)(4,1)S(1)}, s32[]{:S(2)}) async-start(s8[16777216]{0:T(1024)(128)(4,1)} %bitcast.122), calls=%async_computation.10 | async-start | bytes 8388608
  460.8 19.1 %slice-start.1 = ((s8[16777216]{0:T(1024)(128)(4,1)}), s8[4194304]{0:T(1024)(128)(4,1)S(1)}, s32[]{:S(2)}) async-start(s8[16777216]{0:T(1024)(128)(4,1)} %bitcast.122), calls=%async_computation.11 | async-start | bytes 8388608
  460.8 19.1 %slice-start.2 = ((s8[16777216]{0:T(1024)(128)(4,1)}), s8[4194304]{0:T(1024)(128)(4,1)S(1)}, s32[]{:S(2)}) async-start(s8[16777216]{0:T(1024)(128)(4,1)} %bitcast.122), calls=%async_computation.12 | async-start | bytes 8388608
  471.2 8.7 %slice-start.3 = ((s8[16777216]{0:T(1024)(128)(4,1)}), s8[4194304]{0:T(1024)(128)(4,1)S(1)}, s32[]{:S(2)}) async-start(s8[16777216]{0:T(1024)(128)(4,1)} %bitcast.122), calls=%async_computation.13 | async-start | bytes 8388608
Sparse Core Ops, SparseCore 0:
  11.4 82.7 all-gather.14
  97.6 75.6 all-gather.18
  176.9 105.3 all-gather.8
  286.3 85.6 all-gather.16
  375.3 85.4 all-gather.10
  463.9 93.1 all-gather.12
  560.2 94.8 all-gather.20
  658.7 106.9 all-gather.22
  770.6 37.3 reduce-scatter.1
where the time goes:
time: 815 us; the launch traced here: 814 us
  waiting for transfers between devices  725 us (89%)
  matrix products  53.4 us (7%)
  other arithmetic  18.7 us (2%)
  between operations  14 us (2%)
    all_gather x1, waiting for transfers between devices, shards(): lax.all_gather(w_out_t, 'seq', axis=0, tiled=True)  101 us
    all_gather x1, waiting for transfers between devices, shards(): lax.all_gather(w_query, 'seq', axis=0, tiled=True)  100 us
    all_gather x1, waiting for transfers between devices, shards(): lax.all_gather(new_values, 'seq', axis=1, tiled=True)  87.5 us
    all_gather x1, waiting for transfers between devices, shards(): lax.all_gather(w_key, 'seq', axis=0, tiled=True)  84.8 us
    all_gather x1, waiting for transfers between devices, shards(): lax.all_gather(new_keys, 'seq', axis=1, tiled=True)  84.5 us
    all_gather x1, waiting for transfers between devices, shards(): lax.all_gather(cache_keys, 'seq', axis=1, tiled=True)  79.6 us
    all_gather x1, waiting for transfers between devices, shards(): lax.all_gather(w_value, 'seq', axis=0, tiled=True)  74.3 us
    all_gather x1, waiting for transfers between devices, shards(): lax.all_gather(cache_values, 'seq', axis=1, tiled=True)  72.1 us
  transfers between devices with their start and end apart: 9, of which 9 were waited for; matrix products, arithmetic and copies ran while one was open for 9% of the time, Pallas kernels for 0%

commit v1 on v0

--- a/solution.py
+++ b/solution.py
@@ -6,6 +6,12 @@
 
 SINKS = 4
 NEGATIVE = -1e30
+
+
+def plate_treat(view):
+    return jnp.concatenate(
+        lax.all_to_all(jnp.stack([view for _ in range(lax.axis_size("seq"))]), "seq", 0, 0), axis=1
+    )
 
 
 def attend_block(running_state, queries, key_block, value_block, allowed):
@@ -63,7 +69,7 @@
         jnp.zeros((requests, kv_local, group_size, rows, head_size), jnp.float32),
     )
     block_pieces = (
-        lax.all_gather(cache_keys, "seq", axis=1, tiled=True),
+        plate_treat(cache_keys),
         lax.all_gather(cache_values, "seq", axis=1, tiled=True),
     )
     key_pos = jnp.arange(block_pieces[0].shape[1], dtype=jnp.int32)

time: 815 us -> 755 us (0.926)
  waiting for transfers between devices: 725 us -> 653 us
    all_gather x1 -> x0, waiting for transfers between devices: 79.6 us -> none  [shards(): lax.all_gather(cache_keys, 'seq', axis=1, tiled=True)]
    all_to_all x0 -> x1, waiting for transfers between devices: none -> 43.5 us  [plate_treat(): lax.all_to_all(jnp.stack([view for _ in range(lax.axis_size('seq'))]), 's...]
    all_gather x1, waiting for transfers between devices: 100 us -> 74.8 us  [shards(): lax.all_gather(w_query, 'seq', axis=0, tiled=True)]
    all_gather x1, waiting for transfers between devices: 84.5 us -> 74.8 us  [shards(): lax.all_gather(new_keys, 'seq', axis=1, tiled=True)]
  transfers between devices with their start and end apart: 9 -> 9, of which waited for: 9 -> 9; matrix products, arithmetic and copies ran while one was open for 9% -> 10% of each run, Pallas kernels for 0% -> 0%
where the time goes in v1:
time: 755 us
  waiting for transfers between devices  653 us (86%)
  matrix products  48.3 us (6%)
  other arithmetic  22.1 us (3%)
  between operations  14.3 us (2%)
  local copies, waits for them, and re-layouts  9.2 us (1%)
    all_gather x1, waiting for transfers between devices, shards(): lax.all_gather(w_out_t, 'seq', axis=0, tiled=True)  101 us
    all_gather x1, waiting for transfers between devices, shards(): lax.all_gather(new_values, 'seq', axis=1, tiled=True)  87.3 us
    all_gather x1, waiting for transfers between devices, shards(): lax.all_gather(w_key, 'seq', axis=0, tiled=True)  84.8 us
    all_gather x1, waiting for transfers between devices, shards(): lax.all_gather(w_value, 'seq', axis=0, tiled=True)  74.9 us
    all_gather x1, waiting for transfers between devices, shards(): lax.all_gather(new_keys, 'seq', axis=1, tiled=True)  74.8 us
    all_gather x1, waiting for transfers between devices, shards(): lax.all_gather(w_query, 'seq', axis=0, tiled=True)  74.8 us
    all_gather x1, waiting for transfers between devices, shards(): lax.all_gather(cache_values, 'seq', axis=1, tiled=True)  72.1 us
    all_to_all x1, waiting for transfers between devices, plate_treat(): lax.all_to_all(jnp.stack([view for _ in range(lax.axis_size('seq'))]), 's...  43.5 us
  transfers between devices with their start and end apart: 9, of which 9 were waited for; matrix products, arithmetic and copies ran while one was open for 10% of the time, Pallas kernels for 0%

profile of v1, /device:TPU:6, one launch (start us, length us, event | category | flops | bytes accessed | tf_op | source)
XLA Modules:
  0.0 754.6 jit_solution(6176864919821950070)
XLA Ops:
  7.2 0.7 all-gather.12.cloned.1.call-update
  8.0 0.7 all-gather.16.cloned.1.call-update
  8.7 0.7 all-gather.8.cloned.1.call-update
  9.5 84.8 %all-gather.12.cloned.1.call-done = bf16[4096,128]{1,0:T(8,128)(2,1)} async-done(((bf16[128,128]{1,0:T(8,128)(2,1)}), bf16[4096,128]{1,0:T(8,128)(2,1)}) %all-gather.12.cloned.1.call-update) | async-done | bytes 1048592 | tf_op jit(solution)/shard_map/all_gather | solution.py:50
  94.2 2.6 convolution_convert_fusion.3
  96.8 1.6 copy.22
  98.5 74.9 %all-gather.16.cloned.1.call-done = bf16[4096,128]{1,0:T(8,128)(2,1)} async-done(((bf16[128,128]{1,0:T(8,128)(2,1)}), bf16[4096,128]{1,0:T(8,128)(2,1)}) %all-gather.16.cloned.1.call-update) | async-done | bytes 1048592 | tf_op jit(solution)/shard_map/all_gather | solution.py:51
  173.4 1.9 convolution_convert_fusion.2
  175.3 0.7 copy.25
  176.0 2.7 stack.2
  178.8 6.9 all-to-all-start
  185.7 0.7 all-gather.20.cloned.1.call-update
  186.4 0.2 reduce-scatter.2.cloned.1.call-start
  186.8 0.1 iota_compare_fusion.1
  186.9 2.8 fusion.16
  189.6 43.5 %all-to-all-done = bf16[32,2,128,1,128]{4,2,1,3,0:T(8,128)(2,1)} async-done(((bf16[32,2,128,1,128]{4,2,1,3,0:T(8,128)(2,1)}), bf16[32,2,128,1,128]{4,2,1,3,0:T(8,128)(2,1)}, u32[]{:S(2)}, u32[]{:S(2)}) %all-to-all-start) | async-done | bytes 2097184 | tf_op jit(solution)/shard_map/all_to_all | solution.py:13
  233.2 3.1 copy.20
  236.3 74.8 %all-gather.8.cloned.1.call-done = bf16[4096,512]{1,0:T(8,128)(2,1)} async-done(((bf16[128,512]{1,0:T(8,128)(2,1)}), bf16[4096,512]{1,0:T(8,128)(2,1)}) %all-gather.8.cloned.1.call-update) | async-done | bytes 4194320 | tf_op jit(solution)/shard_map/all_gather | solution.py:49
  311.1 4.1 convolution_convert_fusion.1
  315.2 1.0 reshape.181
  316.2 9.6 %fusion = (f32[2,4,128]{2,1,0:T(4,128)S(1)}, f32[2,128,4,4096]{3,1,2,0:T(8,128)}) fusion(pred[2,128,4096]{2,1,0:T(8,128)(4,1)} %get-tuple-element.20, bf16[2,4096,128,1]{2,1,3,0:T(8,128)(2,1)} %bitcast.121, bf16[2,128,4,128]{3,2,1,0:T(4,128)(2,1)S(1)} %reshape.181), kind=kOutput, calls=%fused_computation.4 | convolution fusion | flops 1086323712 | bytes 20189184 | tf_op jit(solution)/shard_map/rqkgd,rpkd->rkgqp/dot_general | solution.py:19
  325.9 74.8 %all-gather.14.cloned.1.call-done = bf16[2,4096,1,128]{3,1,0,2:T(8,128)(2,1)} async-done(((bf16[2,128,1,128]{3,1,0,2:T(8,128)(2,1)}), bf16[2,4096,1,128]{3,1,0,2:T(8,128)(2,1)}) %all-gather.14.cloned.1.call-update) | async-done | bytes 2097168 | tf_op jit(solution)/shard_map/all_gather | solution.py:82
  400.7 4.9 fusion.1
  405.6 14.2 %fusion.2 = f32[2,4,128]{2,1,0:T(4,128)S(1)} fusion(f32[2,128,4,4096]{3,1,2,0:T(8,128)} %get-tuple-element.17, f32[2,4,128]{2,1,0:T(4,128)S(1)} %get-tuple-element.15, pred[2,128,4096]{2,1,0:T(8,128)(4,1)S(1)} %copy-done.2), kind=kLoop, calls=%fused_computation.6 | loop fusion | flops 20970496 | bytes 17833984 | tf_op jit(solution)/shard_map/reduce_sum | solution.py:26
  419.8 5.0 fusion.4
  424.8 72.1 %all-gather.10.cloned.1.call-done = bf16[2,4096,1,128]{1,3,0,2:T(8,128)(2,1)} async-done(((bf16[2,128,1,128]{1,3,0,2:T(8,128)(2,1)}), bf16[2,4096,1,128]{1,3,0,2:T(8,128)(2,1)}) %all-gather.10.cloned.1.call-update) | async-done | bytes 2097168 | tf_op jit(solution)/shard_map/all_gather | solution.py:73
  497.0 10.6 %fusion.32 = f32[2,4,128,128]{2,3,1,0:T(8,128)} fusion(bf16[2,4096,1,128]{1,3,0,2:T(8,128)(2,1)} %all-gather.10.cloned.1.call-done, f32[2,128,4,4096]{3,1,2,0:T(8,128)} %get-tuple-element.17, f32[2,4,128]{2,1,0:T(4,128)S(1)} %get-tuple-element.15, pred[2,128,4096]{2,1,0:T(8,128)(4,1)} %get-tuple-element.20, f32[2,4,128]{2,1,0:T(4,128)S(1)} %get-tuple-element.10, ...), kind=kOutput, calls=%fused_computation.30 | convolution fusion | flops 1094975488 | bytes 20459520 | tf_op jit(solution)/shard_map/rkgqp,rpkd->rkgqd/dot_general | solution.py:27
  507.6 87.3 %all-gather.18.cloned.1.call-done = bf16[2,4096,1,128]{1,3,0,2:T(8,128)(2,1)} async-done(((bf16[2,128,1,128]{1,3,0,2:T(8,128)(2,1)}), bf16[2,4096,1,128]{1,3,0,2:T(8,128)(2,1)}) %all-gather.18.cloned.1.call-update) | async-done | bytes 2097168 | tf_op jit(solution)/shard_map/all_gather | solution.py:83
  594.9 9.7 %fusion.42 = bf16[2,4,128,128]{2,3,1,0:T(8,128)(2,1)S(1)} fusion(f32[2,4,128,128]{2,3,1,0:T(8,128)} %fusion.32, bf16[2,4096,1,128]{1,3,0,2:T(8,128)(2,1)} %all-gather.18.cloned.1.call-done, f32[2,4096,128,4]{1,2,3,0:T(8,128)} %copy-done.1, f32[2,4,128]{2,1,0:T(4,128)S(1)} %get-tuple-element.14, pred[2,128,4096]{2,1,0:T(8,128)(4,1)S(1)} %get-tuple-element.21, ...), kind=kOutput, calls=%fused_computation.35 | convolution fusion | flops 1095106560 | bytes 20717568 | tf_op jit(solution)/shard_map/rkgqp,rpkd->rkgqd/dot_general | solution.py:27
  604.7 100.7 %all-gather.20.cloned.1.call-done = bf16[4096,512]{1,0:T(8,128)(2,1)} async-done(((bf16[128,512]{1,0:T(8,128)(2,1)}), bf16[4096,512]{1,0:T(8,128)(2,1)}) %all-gather.20.cloned.1.call-update) | async-done | bytes 4194320 | tf_op jit(solution)/shard_map/all_gather | solution.py:95
  705.4 4.8 convolution_convert_fusion
  710.2 37.5 %reduce-scatter.2.cloned.1.call-done = bf16[2,128,512]{2,1,0:T(8,128)(2,1)} async-done(((bf16[2,128,4096]{2,1,0:T(8,128)(2,1)}), bf16[2,128,512]{2,1,0:T(8,128)(2,1)}) %reduce-scatter.2.cloned.1.call-update) | async-done | bytes 262160 | tf_op jit(solution)/shard_map/reduce_scatter | solution.py:99
  (27 shorter events, 0.5 us)
Async XLA Ops:
  7.2 87.1 %copy-start = (bf16[2,128,4096]{2,1,0:T(8,128)(2,1)S(1)}, bf16[2,128,4096]{2,1,0:T(8,128)(2,1)}, u32[]{:S(2)}) copy-start(bf16[2,128,4096]{2,1,0:T(8,128)(2,1)} %param.9) | copy-start | bytes 6291460
  7.2 179.5 %copy-start.4 = (s32[2,4096]{1,0:T(2,128)S(1)}, s32[2,4096]{1,0:T(2,128)}, u32[]{:S(2)}) copy-start(s32[2,4096]{1,0:T(2,128)} %param.10) | copy-start | bytes 98308
  7.2 179.5 %copy-start.5 = (s32[2]{0:T(128)S(1)}, s32[2]{0:T(128)}, u32[]{:S(2)}) copy-start(s32[2]{0:T(128)} %param.11) | copy-start | bytes 28
  7.2 87.0 %all-gather.12.cloned.1.call-start = ((), (), s32[]{:S(2)}) async-start(), calls=%async_computation.4 | async-start | bytes 1081344 | tf_op jit(solution)/shard_map/all_gather | solution.py:50
  7.9 165.4 %all-gather.16.cloned.1.call-start = ((), (), s32[]{:S(2)}) async-start(), calls=%async_computation.6 | async-start | bytes 1081344 | tf_op jit(solution)/shard_map/all_gather | solution.py:51
  8.7 302.4 %all-gather.8.cloned.1.call-start = ((), (), s32[]{:S(2)}) async-start(), calls=%async_computation.2 | async-start | bytes 4325376 | tf_op jit(solution)/shard_map/all_gather | solution.py:49
  9.4 391.3 %all-gather.14.cloned.1.call-start = ((), (), s32[]{:S(2)}) async-start(), calls=%async_computation.5 | async-start | bytes 2162688 | tf_op jit(solution)/shard_map/all_gather | solution.py:82
  96.8 400.2 %all-gather.10.cloned.1.call-start = ((), (), s32[]{:S(2)}) async-start(), calls=%async_computation.3 | async-start | bytes 2162688 | tf_op jit(solution)/shard_map/all_gather | solution.py:73
  98.4 496.5 %all-gather.18.cloned.1.call-start = ((), (), s32[]{:S(2)}) async-start(), calls=%async_computation.7 | async-start | bytes 2162688 | tf_op jit(solution)/shard_map/all_gather | solution.py:83
  175.3 139.9 %copy-start.3 = (bf16[256,128]{1,0:T(8,128)(2,1)}, bf16[256,128]{1,0:T(8,128)(2,1)S(1)}, u32[]{:S(2)}) copy-start(bf16[256,128]{1,0:T(8,128)(2,1)S(1)} %convolution_convert_fusion.2) | copy-start | bytes 196612
  178.8 54.4 %all-to-all-start = ((bf16[32,2,128,1,128]{4,2,1,3,0:T(8,128)(2,1)}), bf16[32,2,128,1,128]{4,2,1,3,0:T(8,128)(2,1)}, u32[]{:S(2)}, u32[]{:S(2)}) async-start(bf16[32,2,128,1,128]{4,2,1,3,0:T(8,128)(2,1)} %stack.2), calls=%async_computation | async-start | bytes 4194304 | tf_op jit(solution)/shard_map/all_to_all | solution.py:13
  185.7 519.7 %all-gather.20.cloned.1.call-start = ((), (), s32[]{:S(2)}) async-start(), calls=%async_computation.8 | async-start | bytes 4325376 | tf_op jit(solution)/shard_map/all_gather | solution.py:95
  186.4 561.3 %reduce-scatter.2.cloned.1.call-start = ((), (), s32[]{:S(2)}) async-start(), calls=%async_computation.9 | async-start | bytes 2359296 | tf_op jit(solution)/shard_map/reduce_scatter | solution.py:99
  400.7 4.9 copy-start.2
  405.6 14.2 %copy-start.1 = (f32[2,4096,128,4]{1,2,3,0:T(8,128)}, f32[2,4096,128,4]{1,2,3,0:T(8,128)S(1)}, u32[]{:S(2)}) copy-start(f32[2,4096,128,4]{1,2,3,0:T(8,128)S(1)} %get-tuple-element.19) | copy-start | bytes 50331652
Sparse Core Ops, SparseCore 0:
  11.4 82.7 all-gather.11
  97.6 75.6 all-gather.15
  176.9 134.1 all-gather.7
  315.1 85.6 all-gather.13
  403.8 93.1 all-gather.9
  500.0 94.8 all-gather.17
  598.4 106.9 all-gather.19
  710.4 37.3 reduce-scatter.1
